TPU v7x, 512 devices: a whole 4x4x16 slice. The times are simulated.
512 devices in a mesh: ops: 16 (over x, y), sec: 32 (over z, core).
Axes of the slice: x: 4, y: 4, z: 16, core: 2. Of those that a mesh axis runs over, the one named last changes fastest.
Arguments:
- wave: bfloat16 [32, 768, 768], P('sec')
- left_ops: bfloat16 [16, 32, 768, 768], P('ops', 'sec'), may hold values from -0.21875 to 0.21875
- right_ops: bfloat16 [16, 32, 768, 768], P('ops', 'sec'), may hold values from -0.21875 to 0.21875
- priors: bfloat16 [8, 32, 768, 768], P(None, 'sec', 'ops'), as said below
- row_sizes: int32 [32], P('sec'), may hold values from 64 to 768, as said below
- col_sizes: int32 [32], P('sec'), may hold values from 64 to 768, as said below
Outputs:
- sigma: bfloat16 [32, 768, 768], P('sec', 'ops')
- new_dir: bfloat16 [32, 768, 768], P('sec', 'ops')
- correlations: float32 [8], replicated
Inputs may be any that keep to these rules, and one draw needn't show every extreme that they name: `row_sizes`: one sector's block uses all 768 rows. `col_sizes`: one sector's block uses all 768 columns. `priors`: each prior vector has a norm of about one over all cells.
All inputs are finite; a program needn't handle non-finite values.
Results may differ from a plain program's by a relative error of at most 0.012.
Values sent between devices are 32-bit elements; how exact they have to be, the bound alone decides.
No kernel may reach another device: no remote copies, remote signals or barrier semaphores. Data moves between devices by JAX's collectives and lax.ppermute only.
A program may use at most 64 MiB of HBM per device.

v0:
```python
import jax
import jax.numpy as jnp
from jax import lax
from jax.sharding import PartitionSpec as P


def shards(wave, left_ops, right_ops, priors, row_sizes, col_sizes):
    width = wave.shape[1]
    sec_local = wave.shape[0]
    shard_rows = width // lax.axis_size("ops")
    first_row = lax.axis_index("ops") * shard_rows
    place = jnp.arange(width, dtype=jnp.int32)
    row_mask = (place[None, :] < row_sizes[:, None]).astype(jnp.float32)
    col_mask = (place[None, :] < col_sizes[:, None]).astype(jnp.float32)
    full_mask = row_mask[:, :, None] * col_mask[:, None, :]
    masked = wave * full_mask.astype(jnp.bfloat16)
    inner = jnp.einsum(
        "sab,ksjb->ksaj", masked, right_ops, preferred_element_type=jnp.float32
    ).astype(jnp.bfloat16)
    partial_all = jnp.einsum("ksia,ksaj->sij", left_ops, inner, preferred_element_type=jnp.float32)
    whole = lax.psum(partial_all, "ops")
    summed = lax.dynamic_slice_in_dim(whole, first_row, shard_rows, 1)
    mine_rows = lax.dynamic_slice_in_dim(row_mask, first_row, shard_rows, 1)
    mine_mask = mine_rows[:, :, None] * col_mask[:, None, :]
    sigma = (summed * mine_mask).astype(jnp.bfloat16)
    pmask = (priors * mine_mask[None].astype(jnp.bfloat16)).astype(jnp.float32)
    sig32 = sigma.astype(jnp.float32)
    local_over = jnp.einsum("psab,sab->p", pmask, sig32, precision=lax.Precision.HIGHEST)
    correlations = lax.psum(local_over, ("ops", "sec"))
    resid = sig32 - jnp.einsum("p,psab->sab", correlations, pmask, precision=lax.Precision.HIGHEST)
    total = lax.psum(jnp.sum(resid * resid), ("ops", "sec"))
    cells = sec_local * lax.axis_size("sec") * width * width
    new_dir = (resid / jnp.sqrt(total / cells + 1e-06)).astype(jnp.bfloat16)
    return (sigma, new_dir, correlations)


def solution(mesh):
    in_specs = (
        P("sec", None, None),
        P("ops", "sec", None, None),
        P("ops", "sec", None, None),
        P(None, "sec", "ops", None),
        P("sec"),
        P("sec"),
    )
    out_specs = (P("sec", "ops", None), P("sec", "ops", None), P())
    return jax.shard_map(shards, mesh=mesh, in_specs=in_specs, out_specs=out_specs, check_vma=False)
```

profile of v0, /device:TPU:1, one launch (start us, length us, event | category | flops | bytes accessed | tf_op | source)
XLA Modules:
  0.0 362.4 jit_solution(13174631265643082113)
XLA Ops:
  7.2 0.0 copy-start
  7.2 0.0 all-reduce.2.cloned.1.call-start
  8.6 0.0 copy-done
  8.6 5.6 %convolution_bitcast_fusion = f32[1,768,768]{1,2,0:T(8,128)} fusion(bf16[1,1,768,768]{3,2,1,0:T(8,128)(2,1)S(1)} %copy-done, bf16[1,768,768]{2,1,0:T(8,128)(2,1)} %param.6, bf16[1,1,768,768]{3,2,1,0:T(8,128)(2,1)} %param.8, f32[768]{0:T(1024)S(1)} %get-tuple-element.7, f32[768]{0:T(1024)S(1)} %get-tuple-element.6), kind=kOutput, calls=%fused_computation.1 | convolution fusion | flops 1814298624 | bytes 5904384 | tf_op jit(solution)/shard_map/ksia,ksaj->sij/dot_general | solution.py:20
  14.2 0.0 copy-start.1
  14.2 0.0 all-reduce.2.cloned.1.call-update
  14.2 0.1 multiply_convert_fusion.2
  14.3 0.9 copy-done.1
  15.3 125.8 %all-reduce.2.cloned.1.call-done = f32[1,768,768]{1,2,0:T(8,128)} async-done(((f32[1,768,768]{1,2,0:T(8,128)}), f32[1,768,768]{1,2,0:T(8,128)}) %all-reduce.2.cloned.1.call-update) | async-done | bytes 2359312 | tf_op jit(solution)/shard_map/psum | solution.py:21
  141.1 1.4 fusion.19
  142.5 0.2 copy.12
  142.7 0.5 convolution_bitcast_fusion.1
  143.2 105.0 %psum.22 = f32[8]{0:T(128)S(1)} all-reduce(f32[8]{0:T(128)S(1)} %convolution_bitcast_fusion.1), channel_id=1, replica_groups=mesh['ops'=16,'sec'=32] {'ops','sec'}, use_global_device_ids=true, to_apply=%region_1.0 | all-reduce | flops 8 | bytes 64 | tf_op jit(solution)/shard_map/psum | solution.py:29
  248.2 0.0 copy-start.2
  248.2 0.6 fusion.11
  248.8 0.2 copy.13
  249.0 1.4 multiply_convert_fusion.1
  250.4 2.0 multiply_reduce_fusion
  252.4 0.0 copy-done.2
  252.4 0.8 copy.9
  253.2 99.5 %psum.23 = f32[]{:T(128)} all-reduce(f32[]{:T(128)} %multiply_reduce_fusion), channel_id=1, replica_groups=mesh['ops'=16,'sec'=32] {'ops','sec'}, use_global_device_ids=true, to_apply=%region_3.0 | all-reduce | flops 1 | bytes 8 | tf_op jit(solution)/shard_map/psum | solution.py:31
  353.4 1.4 divide_convert_fusion
  354.8 0.8 copy.10
  (3 shorter events, 0.1 us)
Async XLA Ops:
  7.2 1.5 copy-start
  7.2 133.9 %all-reduce.2.cloned.1.call-start = ((), (), s32[]{:S(2)}) async-start(), calls=%async_computation | async-start | bytes 4718592 | tf_op jit(solution)/shard_map/psum | solution.py:21
  14.2 1.1 copy-start.1
  248.2 4.3 %copy-start.2 = (f32[8]{0:T(128)}, f32[8]{0:T(128)S(1)}, u32[]{:S(2)}) copy-start(f32[8]{0:T(128)S(1)} %psum.22) | copy-start | bytes 100
Sparse Core Ops, SparseCore 0:
  14.3 126.6 all-reduce.1
where the time goes:
time: 363 us; the launch traced here: 362 us
  blocking collectives  204 us (56%)
  waiting for transfers between devices  126 us (35%)
  between operations  16.2 us (4%)
  matrix products  6.72 us (2%)
  other arithmetic  6.38 us (2%)
    psum x1, waiting for transfers between devices, shards(): whole = lax.psum(partial_all, 'ops')  126 us
    psum x1, blocking collectives, shards(): correlations = lax.psum(local_over, ('ops', 'sec'))  105 us
    psum x1, blocking collectives, shards(): total = lax.psum(jnp.sum(resid * resid), ('ops', 'sec'))  99.5 us
  transfers between devices with their start and end apart: 1, of which 1 were waited for; matrix products, arithmetic and copies ran while one was open for 0% of the time, Pallas kernels for 0%

commit v1 on v0

--- a/solution.py
+++ b/solution.py
@@ -18,7 +18,9 @@
         "sab,ksjb->ksaj", masked, right_ops, preferred_element_type=jnp.float32
     ).astype(jnp.bfloat16)
     partial_all = jnp.einsum("ksia,ksaj->sij", left_ops, inner, preferred_element_type=jnp.float32)
-    whole = lax.psum(partial_all, "ops")
+    whole = partial_all
+    for hop in (1, 2, 4, 8):
+        whole = whole + lax.ppermute(whole, "ops", [(dev, dev ^ hop) for dev in range(16)])
     summed = lax.dynamic_slice_in_dim(whole, first_row, shard_rows, 1)
     mine_rows = lax.dynamic_slice_in_dim(row_mask, first_row, shard_rows, 1)
     mine_mask = mine_rows[:, :, None] * col_mask[:, None, :]

time: 363 us -> 441 us (1.21)
  waiting for transfers between devices: 126 us -> 193 us
  starting transfers between devices: 0.04 us -> 21.1 us
  between operations: 16.2 us -> 2.84 us
  blocking collectives: 204 us -> 211 us
    ppermute x0 -> x4, waiting for transfers between devices: none -> 193 us  [shards(): lax.ppermute(whole, 'ops', [(dev, dev ^ hop) for dev in range(16)])]
    psum x1 -> x0, waiting for transfers between devices: 126 us -> none  [shards(): whole = lax.psum(partial_all, 'ops')]
    ppermute x0 -> x4, starting transfers between devices: none -> 21.1 us  [shards(): lax.ppermute(whole, 'ops', [(dev, dev ^ hop) for dev in range(16)])]
    psum x1, blocking collectives: 105 us -> 111 us  [shards(): correlations = lax.psum(local_over, ('ops', 'sec'))]
  transfers between devices with their start and end apart: 1 -> 4, of which waited for: 1 -> 4; matrix products, arithmetic and copies ran while one was open for 0% -> 0% of each run, Pallas kernels for 0% -> 0%
where the time goes in v1:
time: 441 us; the launch traced here: 440 us
  blocking collectives  211 us (48%)
  waiting for transfers between devices  193 us (44%)
  starting transfers between devices  21.1 us (5%)
  other arithmetic  6.16 us (1%)
  matrix products  5.88 us (1%)
    ppermute x4, waiting for transfers between devices, shards(): lax.ppermute(whole, 'ops', [(dev, dev ^ hop) for dev in range(16)])  193 us
    psum x1, blocking collectives, shards(): correlations = lax.psum(local_over, ('ops', 'sec'))  111 us
    psum x1, blocking collectives, shards(): total = lax.psum(jnp.sum(resid * resid), ('ops', 'sec'))  99.3 us
    ppermute x4, starting transfers between devices, shards(): lax.ppermute(whole, 'ops', [(dev, dev ^ hop) for dev in range(16)])  21.1 us
  transfers between devices with their start and end apart: 4, of which 4 were waited for; matrix products, arithmetic and copies ran while one was open for 0% of the time, Pallas kernels for 0%

profile of v1, /device:TPU:1, one launch (start us, length us, event | category | flops | bytes accessed | tf_op | source)
XLA Modules:
  0.0 440.2 jit_solution(13895180917017884375)
XLA Ops:
  0.6 0.0 copy-start
  2.0 0.0 copy-done
  2.1 3.7 convolution_bitcast_fusion
  5.7 4.0 collective-permute-start
  9.8 46.1 %collective-permute-done = f32[1,768,768]{2,1,0:T(8,128)S(1)} collective-permute-done((f32[1,768,768]{2,1,0:T(8,128)S(1)}, f32[1,768,768]{2,1,0:T(8,128)S(1)}, u32[]{:S(2)}, u32[]{:S(2)}) %collective-permute-start) | collective-permute-done | bytes 2359328 | tf_op jit(solution)/shard_map/ppermute | solution.py:23
  55.9 0.3 add.23
  56.2 9.5 %collective-permute-start.1 = (f32[1,768,768]{2,1,0:T(8,128)S(1)}, f32[1,768,768]{2,1,0:T(8,128)S(1)}, u32[]{:S(2)}, u32[]{:S(2)}) collective-permute-start(f32[1,768,768]{2,1,0:T(8,128)S(1)} %add.23), channel_id=1, source_target_pairs={{0,64},{32,96},{64,0},{96,32},{128,192},{160,224},{192,128},{224,1... | collective-permute-start | bytes 7077896 | tf_op jit(solution)/shard_map/ppermute | solution.py:23
  65.7 49.9 %collective-permute-done.1 = f32[1,768,768]{2,1,0:T(8,128)S(1)} collective-permute-done((f32[1,768,768]{2,1,0:T(8,128)S(1)}, f32[1,768,768]{2,1,0:T(8,128)S(1)}, u32[]{:S(2)}, u32[]{:S(2)}) %collective-permute-start.1) | collective-permute-done | bytes 2359328 | tf_op jit(solution)/shard_map/ppermute | solution.py:23
  115.6 0.3 add.24
  115.9 3.1 collective-permute-start.2
  119.0 49.4 %collective-permute-done.2 = f32[1,768,768]{2,1,0:T(8,128)S(1)} collective-permute-done((f32[1,768,768]{2,1,0:T(8,128)S(1)}, f32[1,768,768]{2,1,0:T(8,128)S(1)}, u32[]{:S(2)}, u32[]{:S(2)}) %collective-permute-start.2) | collective-permute-done | bytes 2359328 | tf_op jit(solution)/shard_map/ppermute | solution.py:23
  168.4 0.3 add.25
  168.7 4.5 %collective-permute-start.3 = (f32[1,768,768]{2,1,0:T(8,128)S(1)}, f32[1,768,768]{2,1,0:T(8,128)}, u32[]{:S(2)}, u32[]{:S(2)}) collective-permute-start(f32[1,768,768]{2,1,0:T(8,128)S(1)} %add.25), channel_id=1, source_target_pairs={{0,256},{32,288},{64,320},{96,352},{128,384},{160,416},{192,448},{... | collective-permute-start | bytes 7077896 | tf_op jit(solution)/shard_map/ppermute | solution.py:23
  173.2 0.1 multiply_convert_fusion.1
  173.2 1.1 multiply_bitcast_fusion
  174.4 0.0 copy-start.1
  174.4 47.5 %collective-permute-done.3 = f32[1,768,768]{2,1,0:T(8,128)} collective-permute-done((f32[1,768,768]{2,1,0:T(8,128)S(1)}, f32[1,768,768]{2,1,0:T(8,128)}, u32[]{:S(2)}, u32[]{:S(2)}) %collective-permute-start.3) | collective-permute-done | bytes 2359328 | tf_op jit(solution)/shard_map/ppermute | solution.py:23
  221.8 1.0 fusion.15
  222.8 0.0 copy-start.2
  222.8 0.0 copy-done.1
  222.9 0.6 copy-done.2
  223.5 0.5 convolution_bitcast_fusion.1
  224.0 111.4 %psum.14 = f32[8]{0:T(128)S(1)} all-reduce(f32[8]{0:T(128)S(1)} %convolution_bitcast_fusion.1), channel_id=1, replica_groups=mesh['ops'=16,'sec'=32] {'ops','sec'}, use_global_device_ids=true, to_apply=%region_0.0 | all-reduce | flops 8 | bytes 64 | tf_op jit(solution)/shard_map/psum | solution.py:31
  335.4 0.0 copy-start.3
  335.4 1.7 fusion.11
  337.1 1.5 multiply_reduce_fusion
  338.7 99.3 %psum.15 = f32[]{:T(128)} all-reduce(f32[]{:T(128)} %multiply_reduce_fusion), channel_id=1, replica_groups=mesh['ops'=16,'sec'=32] {'ops','sec'}, use_global_device_ids=true, to_apply=%region_2.0 | all-reduce | flops 1 | bytes 8 | tf_op jit(solution)/shard_map/psum | solution.py:33
  438.7 1.5 divide_convert_fusion
  440.2 0.0 copy-done.3
  (2 shorter events, 0.0 us)
Async XLA Ops:
  0.6 1.4 copy-start
  5.7 50.2 %collective-permute-start = (f32[1,768,768]{2,1,0:T(8,128)S(1)}, f32[1,768,768]{2,1,0:T(8,128)S(1)}, u32[]{:S(2)}, u32[]{:S(2)}) collective-permute-start(f32[1,768,768]{2,1,0:T(8,128)S(1)} %convolution_bitcast_fusion), channel_id=1, source_target_pairs={{0,32},{32,0},{64,96},{96,64},{128,160},{160,128},{192,224},{224,1... | collective-permute-start | bytes 7077896 | tf_op jit(solution)/shard_map/ppermute | solution.py:23
  56.2 59.4 %collective-permute-start.1 = (f32[1,768,768]{2,1,0:T(8,128)S(1)}, f32[1,768,768]{2,1,0:T(8,128)S(1)}, u32[]{:S(2)}, u32[]{:S(2)}) collective-permute-start(f32[1,768,768]{2,1,0:T(8,128)S(1)} %add.23), channel_id=1, source_target_pairs={{0,64},{32,96},{64,0},{96,32},{128,192},{160,224},{192,128},{224,1... | collective-permute-start | bytes 7077896 | tf_op jit(solution)/shard_map/ppermute | solution.py:23
  115.9 52.4 %collective-permute-start.2 = (f32[1,768,768]{2,1,0:T(8,128)S(1)}, f32[1,768,768]{2,1,0:T(8,128)S(1)}, u32[]{:S(2)}, u32[]{:S(2)}) collective-permute-start(f32[1,768,768]{2,1,0:T(8,128)S(1)} %add.24), channel_id=1, source_target_pairs={{0,128},{32,160},{64,192},{96,224},{128,0},{160,32},{192,64},{224,... | collective-permute-start | bytes 7077896 | tf_op jit(solution)/shard_map/ppermute | solution.py:23
  168.7 53.2 %collective-permute-start.3 = (f32[1,768,768]{2,1,0:T(8,128)S(1)}, f32[1,768,768]{2,1,0:T(8,128)}, u32[]{:S(2)}, u32[]{:S(2)}) collective-permute-start(f32[1,768,768]{2,1,0:T(8,128)S(1)} %add.25), channel_id=1, source_target_pairs={{0,256},{32,288},{64,320},{96,352},{128,384},{160,416},{192,448},{... | collective-permute-start | bytes 7077896 | tf_op jit(solution)/shard_map/ppermute | solution.py:23
  174.4 48.5 %copy-start.1 = (bf16[8,48,768]{2,1,0:T(8,128)(2,1)}, bf16[8,48,768]{2,1,0:T(8,128)(2,1)S(1)}, u32[]{:S(2)}) copy-start(bf16[8,48,768]{2,1,0:T(8,128)(2,1)S(1)} %multiply_bitcast_fusion) | copy-start | bytes 1769476
  222.8 0.6 copy-start.2
  335.4 104.8 %copy-start.3 = (f32[8]{0:T(128)}, f32[8]{0:T(128)S(1)}, u32[]{:S(2)}) copy-start(f32[8]{0:T(128)S(1)} %psum.14) | copy-start | bytes 100
